TPU v7x, 32 devices: a whole 2x2x4 slice. The times are simulated.
32 devices in a mesh: row: 8 (over z, core), col: 4 (over y, x).
Axes of the slice: x: 2, y: 2, z: 4, core: 2. Of those that a mesh axis runs over, the one named last changes fastest.
Arguments:
- activations: bfloat16 [1024, 8192], P('col', 'row'), may hold values from -6 to 6
- out_grad: bfloat16 [1024, 8192], P('col', 'row'), may hold values from -6 to 6
- gate_pre: bfloat16 [1024, 16384], P('row', 'col'), may hold values from -8 to 8
- up_proj: bfloat16 [1024, 16384], P('row', 'col'), may hold values from -6 to 6
- gate_weight: bfloat16 [8192, 16384], P('row', 'col'), may hold values from -0.0625 to 0.0625
- up_weight: bfloat16 [8192, 16384], P('row', 'col'), may hold values from -0.0625 to 0.0625
- down_weight: bfloat16 [16384, 8192], P('col', 'row'), may hold values from -0.046875 to 0.046875
Outputs:
- input_grad: bfloat16 [1024, 8192], P('col', 'row')
- gate_grad: bfloat16 [8192, 16384], P('row', 'col')
- up_grad: bfloat16 [8192, 16384], P('row', 'col')
- down_grad: bfloat16 [16384, 8192], P('col', 'row')
All inputs are finite; a program needn't handle non-finite values.
Results may differ from a plain program's by a relative error of at most 0.0051.
Values may be sent and summed in bfloat16 or wider, within the bound.
No kernel may reach another device: no remote copies, remote signals or barrier semaphores. Data moves between devices by JAX's collectives and lax.ppermute only.
A program may use at most 192 MiB of HBM per device.

v0:
```python
import jax
import jax.numpy as jnp
from jax import lax
from jax.sharding import PartitionSpec as P

CONTRACT_LAST = (((1,), (1,)), ((), ()))
CONTRACT_FIRST = (((0,), (0,)), ((), ()))
ROW = ("z", "core")


def shift_perm(n, s):
    return [(i, (i + s) % n) for i in range(n)]


def gather_col(block):
    n = lax.axis_size("col")
    c = lax.axis_index("col")
    rows = block.shape[0]
    full = jnp.zeros((n * rows,) + block.shape[1:], block.dtype)
    full = lax.dynamic_update_slice_in_dim(full, block, c * rows, axis=0)
    for s in range(1, n):
        part = lax.ppermute(block, "col", shift_perm(n, s))
        full = lax.dynamic_update_slice_in_dim(full, part, (c - s) % n * rows, axis=0)
    return full


def reduce_scatter_col(partial, send_dtype=jnp.float32):
    n = lax.axis_size("col")
    c = lax.axis_index("col")
    blocks = partial.reshape((n, -1) + partial.shape[1:])
    total = lax.dynamic_index_in_dim(blocks, c, axis=0, keepdims=False)
    for s in range(1, n):
        piece = lax.dynamic_index_in_dim(blocks, (c + s) % n, axis=0, keepdims=False)
        piece = lax.ppermute(piece.astype(send_dtype), "col", shift_perm(n, s))
        total = total + piece.astype(jnp.float32)
    return total


def body(activations, out_grad, gate_pre, up_proj, gate_weight, up_weight, down_weight):
    gate_float = gate_pre.astype(jnp.float32)
    up_float = up_proj.astype(jnp.float32)
    sigmoid_gate = jax.nn.sigmoid(gate_float)
    silu_gate = gate_float * sigmoid_gate
    hidden_local = (silu_gate * up_float).astype(jnp.bfloat16)
    hidden_act = lax.all_gather(hidden_local, ROW, axis=0, tiled=True)
    grad_full = gather_col(out_grad)
    activations, grad_full = lax.optimization_barrier((activations, grad_full))
    act_full = gather_col(activations)
    tokens_all = act_full.shape[0]
    chips = lax.axis_size("z")
    z = lax.axis_index("z")
    core = lax.axis_index("core")
    width = grad_full.shape[1]
    grad_blocks = grad_full.reshape(chips, 2, -1, width)
    grad_send = lax.dynamic_index_in_dim(grad_blocks, 1 - core, axis=1, keepdims=False)
    grad_keep = lax.dynamic_index_in_dim(grad_blocks, core, axis=1, keepdims=False)
    hid_send = lax.dot_general(
        grad_send.reshape(-1, width), down_weight, CONTRACT_LAST, preferred_element_type=jnp.float32
    )
    hid_recv = lax.ppermute(hid_send, "core", [(0, 1), (1, 0)])
    hid_keep = lax.dot_general(
        grad_keep.reshape(-1, width), down_weight, CONTRACT_LAST, preferred_element_type=jnp.float32
    )
    chip_sum = (hid_keep + hid_recv).reshape(chips, -1, hid_keep.shape[1])
    chip_sum, hidden_act, act_full = lax.optimization_barrier((chip_sum, hidden_act, act_full))
    hid_rows = lax.dynamic_index_in_dim(chip_sum, z, axis=0, keepdims=False)
    for s in [1] + list(range(chips - 1, 1, -1)):
        piece = lax.dynamic_index_in_dim(chip_sum, (z + s) % chips, axis=0, keepdims=False)
        piece = lax.ppermute(piece.astype(jnp.bfloat16), "z", shift_perm(chips, s))
        hid_rows = hid_rows + piece.astype(jnp.float32)
    gate_local = (
        hid_rows * up_float * sigmoid_gate * (1.0 + gate_float * (1.0 - sigmoid_gate))
    ).astype(jnp.bfloat16)
    gate_local, hid_rows = lax.optimization_barrier((gate_local, hid_rows))
    up_local = (hid_rows * silu_gate).astype(jnp.bfloat16)
    acc_down = lax.dot_general(
        hidden_act, grad_full, CONTRACT_FIRST, preferred_element_type=jnp.float32
    )
    gate_delta = lax.all_gather(gate_local, ROW, axis=0, tiled=True)
    up_delta = lax.all_gather(up_local, ROW, axis=0, tiled=True)
    acc_gate = lax.dot_general(
        act_full, gate_delta, CONTRACT_FIRST, preferred_element_type=jnp.float32
    )
    input_gate = reduce_scatter_col(
        lax.dot_general(gate_delta, gate_weight, CONTRACT_LAST, preferred_element_type=jnp.float32)
    )
    acc_gate, input_gate, up_delta = lax.optimization_barrier((acc_gate, input_gate, up_delta))
    input_up = lax.dot_general(
        up_delta, up_weight, CONTRACT_LAST, preferred_element_type=jnp.float32
    )
    up_delta, input_up = lax.optimization_barrier((up_delta, input_up))
    input_up = reduce_scatter_col(input_up, jnp.bfloat16)
    acc_up = lax.dot_general(act_full, up_delta, CONTRACT_FIRST, preferred_element_type=jnp.float32)
    input_rows = (input_gate + input_up).astype(jnp.bfloat16)
    factor = float(tokens_all) ** (-0.5)
    return (
        input_rows,
        (acc_gate * factor).astype(jnp.bfloat16),
        (acc_up * factor).astype(jnp.bfloat16),
        (acc_down * factor).astype(jnp.bfloat16),
    )


def solution(mesh):
    in_specs = (
        P("col", ROW),
        P("col", ROW),
        P(ROW, "col"),
        P(ROW, "col"),
        P(ROW, "col"),
        P(ROW, "col"),
        P("col", ROW),
    )
    out_specs = (P("col", ROW), P(ROW, "col"), P(ROW, "col"), P("col", ROW))
    devices = mesh.devices.reshape(mesh.shape["row"] // 2, 2, mesh.shape["col"])
    split_mesh = jax.sharding.Mesh(devices, ("z", "core", "col"))
    return jax.shard_map(
        body, mesh=split_mesh, in_specs=in_specs, out_specs=out_specs, check_vma=False
    )
```

profile of v0, /device:TPU:0, one launch (start us, length us, event | category | flops | bytes accessed | tf_op | source)
XLA Modules:
  0.0 409.8 jit_solution(13424678668484892783)
XLA Ops:
  7.2 3.2 fusion
  10.5 3.0 collective-permute-start
  16.8 10.6 %collective-permute-done = bf16[256,1024]{1,0:T(8,128)(2,1)} collective-permute-done((bf16[256,1024]{1,0:T(8,128)(2,1)S(1)}, bf16[256,1024]{1,0:T(8,128)(2,1)}, u32[]{:S(2)}, u32[]{:S(2)}) %collective-permute-start) | collective-permute-done | bytes 524320 | tf_op jit(solution)/shard_map/ppermute | solution.py:22
  28.4 9.3 %collective-permute-done.1 = bf16[256,1024]{1,0:T(8,128)(2,1)} collective-permute-done((bf16[256,1024]{1,0:T(8,128)(2,1)S(1)}, bf16[256,1024]{1,0:T(8,128)(2,1)}, u32[]{:S(2)}, u32[]{:S(2)}) %collective-permute-start.1) | collective-permute-done | bytes 524320 | tf_op jit(solution)/shard_map/ppermute | solution.py:22
  39.1 6.8 %fusion.23 = f32[512,4096]{1,0:T(8,128)} fusion(bf16[512,1024]{1,0:T(8,128)(2,1)S(1)} %bitcast.71, bf16[4096,1024]{1,0:T(8,128)(2,1)S(1)} %copy-done.2), kind=kOutput, calls=%fused_computation.54 | convolution fusion | flops 4294967296 | bytes 17825792 | tf_op jit(solution)/shard_map/dot_general | solution.py:57
  45.9 2.0 collective-permute-start.4
  48.3 2.3 collective-permute-start.6
  52.2 1.9 constant_dynamic-update-slice_fusion.3
  54.0 7.9 %collective-permute-done.4 = bf16[256,1024]{1,0:T(8,128)(2,1)} collective-permute-done((bf16[256,1024]{1,0:T(8,128)(2,1)}, bf16[256,1024]{1,0:T(8,128)(2,1)}, u32[]{:S(2)}, u32[]{:S(2)}) %collective-permute-start.4) | collective-permute-done | bytes 524320 | tf_op jit(solution)/shard_map/ppermute | solution.py:22
  61.9 1.9 constant_dynamic-update-slice_fusion.2
  63.8 8.9 %collective-permute-done.5 = bf16[256,1024]{1,0:T(8,128)(2,1)} collective-permute-done((bf16[256,1024]{1,0:T(8,128)(2,1)}, bf16[256,1024]{1,0:T(8,128)(2,1)}, u32[]{:S(2)}, u32[]{:S(2)}) %collective-permute-start.5) | collective-permute-done | bytes 524320 | tf_op jit(solution)/shard_map/ppermute | solution.py:22
  72.7 1.9 constant_dynamic-update-slice_fusion.1
  74.6 1.9 constant_dynamic-update-slice_fusion
  76.4 11.5 %convolution_add_fusion = f32[512,4096]{1,0:T(8,128)} fusion(f32[512,4096]{1,0:T(8,128)} %collective-permute-done.3, bf16[512,1024]{1,0:T(8,128)(2,1)S(1)} %bitcast.70, bf16[4096,1024]{1,0:T(8,128)(2,1)} %param.13), kind=kOutput, calls=%fused_computation.3 | convolution fusion | flops 4297064448 | bytes 26214400 | tf_op jit(solution)/shard_map/dot_general | solution.py:61
  88.0 7.4 %all-gather.4.cloned.1.call-done = bf16[1024,4096]{1,0:T(8,128)(2,1)} async-done(((bf16[128,4096]{1,0:T(8,128)(2,1)}), bf16[1024,4096]{1,0:T(8,128)(2,1)}) %all-gather.4.cloned.1.call-update) | async-done | bytes 8388624 | tf_op jit(solution)/shard_map/all_gather | solution.py:45
  95.3 4.7 %fusion.10 = (bf16[128,4096]{1,0:T(8,128)(2,1)}, bf16[128,4096]{1,0:T(8,128)(2,1)}, bf16[128,4096]{1,0:T(8,128)(2,1)}) fusion(f32[4,128,4096]{2,1,0:T(8,128)} %bitcast.66, s32[]{:T(128)S(6)} %select_n.115, s32[]{:T(128)S(6)} %select_n.119, s32[]{:T(128)S(6)} %select_n.117), kind=kLoop, calls=%fused_computation.24 | loop fusion | bytes 6291468 | tf_op jit(solution)/shard_map/convert_element_type | solution.py:69
  101.2 2.7 collective-permute-start.8
  103.9 24.4 %collective-permute-done.7 = bf16[128,4096]{1,0:T(8,128)(2,1)} collective-permute-done((bf16[128,4096]{1,0:T(8,128)(2,1)}, bf16[128,4096]{1,0:T(8,128)(2,1)}, u32[]{:S(2)}, u32[]{:S(2)}) %collective-permute-start.7) | collective-permute-done | bytes 1048608 | tf_op jit(solution)/shard_map/ppermute | solution.py:69
  128.3 43.9 %collective-permute-done.9 = bf16[128,4096]{1,0:T(8,128)(2,1)} collective-permute-done((bf16[128,4096]{1,0:T(8,128)(2,1)}, bf16[128,4096]{1,0:T(8,128)(2,1)}, u32[]{:S(2)}, u32[]{:S(2)}) %collective-permute-start.9) | collective-permute-done | bytes 1048608 | tf_op jit(solution)/shard_map/ppermute | solution.py:69
  172.3 5.8 %fusion.3 = (bf16[128,4096]{1,0:T(8,128)(2,1)}, f32[128,4096]{1,0:T(8,128)}) fusion(bf16[128,4096]{1,0:T(8,128)(2,1)} %param.10, bf16[128,4096]{1,0:T(8,128)(2,1)S(1)} %copy-done, bf16[128,4096]{1,0:T(8,128)(2,1)} %collective-permute-done.9, bf16[128,4096]{1,0:T(8,128)(2,1)} %collective-permute-done.8, bf16[128,4096]{1,0:T(8,128)(2,1)} %collective-permute-done.7, ...), kind=kLoop, calls=%fused_computation.12 | loop fusion | flops 9437184 | bytes 10485764 | tf_op jit(solution)/shard_map/convert_element_type | solution.py:73
  178.4 3.2 multiply_convert_fusion.3
  181.6 14.6 %multiply_convert_fusion = bf16[4096,1024]{1,0:T(8,128)(2,1)} fusion(bf16[1024,4096]{1,0:T(8,128)(2,1)} %all-gather.4.cloned.1.call-done, bf16[1024,1024]{1,0:T(8,128)(2,1)S(1)} %constant_dynamic-update-slice_fusion.4), kind=kOutput, calls=%fused_computation | convolution fusion | flops 8598323200 | bytes 18874368 | tf_op jit(solution)/shard_map/dot_general | solution.py:76
  196.2 84.4 %all-gather.6.cloned.1.call-done = bf16[1024,4096]{1,0:T(8,128)(2,1)} async-done(((bf16[128,4096]{1,0:T(8,128)(2,1)}), bf16[1024,4096]{1,0:T(8,128)(2,1)}) %all-gather.6.cloned.1.call-update) | async-done | bytes 8388624 | tf_op jit(solution)/shard_map/all_gather | solution.py:79
  280.6 12.8 %fusion.25 = f32[1024,1024]{1,0:T(8,128)S(1)} fusion(bf16[1024,4096]{1,0:T(8,128)(2,1)} %all-gather.6.cloned.1.call-done, bf16[1024,4096]{1,0:T(8,128)(2,1)} %param.11), kind=kOutput, calls=%fused_computation.56 | convolution fusion | flops 8589934592 | bytes 20971520 | tf_op jit(solution)/shard_map/dot_general | solution.py:85
  298.2 13.7 %fusion.24 = f32[1024,4096]{1,0:T(8,128)} fusion(bf16[1024,1024]{1,0:T(8,128)(2,1)} %constant_dynamic-update-slice_fusion, bf16[1024,4096]{1,0:T(8,128)(2,1)S(1)} %copy-done.3), kind=kOutput, calls=%fused_computation.55 | convolution fusion | flops 8589934592 | bytes 27262976 | tf_op jit(solution)/shard_map/dot_general | solution.py:81
  311.9 8.8 %collective-permute-done.10 = f32[256,1024]{1,0:T(8,128)S(1)} collective-permute-done((f32[256,1024]{1,0:T(8,128)S(1)}, f32[256,1024]{1,0:T(8,128)S(1)}, u32[]{:S(2)}, u32[]{:S(2)}) %collective-permute-start.10) | collective-permute-done | bytes 1048608 | tf_op jit(solution)/shard_map/ppermute | solution.py:34
  320.7 21.8 %collective-permute-done.12 = f32[256,1024]{1,0:T(8,128)S(1)} collective-permute-done((f32[256,1024]{1,0:T(8,128)S(1)}, f32[256,1024]{1,0:T(8,128)S(1)}, u32[]{:S(2)}, u32[]{:S(2)}) %collective-permute-start.12) | collective-permute-done | bytes 1048608 | tf_op jit(solution)/shard_map/ppermute | solution.py:34
  342.9 19.9 %all-gather.8.cloned.1.call-done = bf16[1024,4096]{1,0:T(8,128)(2,1)} async-done(((bf16[128,4096]{1,0:T(8,128)(2,1)}), bf16[1024,4096]{1,0:T(8,128)(2,1)}) %all-gather.8.cloned.1.call-update) | async-done | bytes 8388624 | tf_op jit(solution)/shard_map/all_gather | solution.py:80
  362.8 12.6 %fusion.26 = f32[1024,1024]{1,0:T(8,128)S(1)} fusion(bf16[1024,4096]{1,0:T(8,128)(2,1)} %all-gather.8.cloned.1.call-done, bf16[1024,4096]{1,0:T(8,128)(2,1)} %param.12), kind=kOutput, calls=%fused_computation.57 | convolution fusion | flops 8589934592 | bytes 20971520 | tf_op jit(solution)/shard_map/dot_general | solution.py:88
  380.3 15.6 %multiply_convert_fusion.1 = bf16[1024,4096]{1,0:T(8,128)(2,1)} fusion(bf16[1024,1024]{1,0:T(8,128)(2,1)} %constant_dynamic-update-slice_fusion, bf16[1024,4096]{1,0:T(8,128)(2,1)} %all-gather.8.cloned.1.call-done), kind=kOutput, calls=%fused_computation.1 | convolution fusion | flops 8598323200 | bytes 18874368 | tf_op jit(solution)/shard_map/dot_general | solution.py:93
  395.9 4.0 multiply_convert_fusion.2
  399.9 2.2 collective-permute-done.15
  (53 shorter events, 20.3 us)
Async XLA Ops:
  7.2 3.3 copy-start.1
  7.2 88.2 %all-gather.4.cloned.1.call-start = ((), (), s32[]{:S(2)}) async-start(), calls=%async_computation | async-start | bytes 9437184 | tf_op jit(solution)/shard_map/all_gather | solution.py:45
  10.4 270.2 %all-gather.6.cloned.1.call-start = ((), (), s32[]{:S(2)}) async-start(), calls=%async_computation.1 | async-start | bytes 9437184 | tf_op jit(solution)/shard_map/all_gather | solution.py:79
  10.5 16.8 %collective-permute-start = (bf16[256,1024]{1,0:T(8,128)(2,1)S(1)}, bf16[256,1024]{1,0:T(8,128)(2,1)}, u32[]{:S(2)}, u32[]{:S(2)}) collective-permute-start(bf16[256,1024]{1,0:T(8,128)(2,1)S(1)} %copy-done.1), channel_id=1, source_target_pairs={{0,1},{1,2},{2,3},{3,0},{4,5},{5,6},{6,7},{7,4},{8,9},{9,10},{10,1... | collective-permute-start | bytes 1572872 | tf_op jit(solution)/shard_map/ppermute | solution.py:22
  13.5 24.2 %collective-permute-start.1 = (bf16[256,1024]{1,0:T(8,128)(2,1)S(1)}, bf16[256,1024]{1,0:T(8,128)(2,1)}, u32[]{:S(2)}, u32[]{:S(2)}) collective-permute-start(bf16[256,1024]{1,0:T(8,128)(2,1)S(1)} %copy-done.1), channel_id=1, source_target_pairs={{0,2},{1,3},{2,0},{3,1},{4,6},{5,7},{6,4},{7,5},{8,10},{9,11},{10,... | collective-permute-start | bytes 1572872 | tf_op jit(solution)/shard_map/ppermute | solution.py:22
  15.0 23.8 %collective-permute-start.2 = (bf16[256,1024]{1,0:T(8,128)(2,1)S(1)}, bf16[256,1024]{1,0:T(8,128)(2,1)S(1)}, u32[]{:S(2)}, u32[]{:S(2)}) collective-permute-start(bf16[256,1024]{1,0:T(8,128)(2,1)S(1)} %copy-done.1), channel_id=1, source_target_pairs={{0,3},{1,0},{2,1},{3,2},{4,7},{5,4},{6,5},{7,6},{8,11},{9,8},{10,9... | collective-permute-start | bytes 1572872 | tf_op jit(solution)/shard_map/ppermute | solution.py:22
  16.7 22.4 %copy-start.2 = (bf16[4096,1024]{1,0:T(8,128)(2,1)S(1)}, bf16[4096,1024]{1,0:T(8,128)(2,1)}, u32[]{:S(2)}) copy-start(bf16[4096,1024]{1,0:T(8,128)(2,1)} %param.13) | copy-start | bytes 25165828
  45.9 30.5 %collective-permute-start.3 = (f32[512,4096]{1,0:T(8,128)}, f32[512,4096]{1,0:T(8,128)}, u32[]{:S(2)}, u32[]{:S(2)}) collective-permute-start(f32[512,4096]{1,0:T(8,128)} %fusion.23), channel_id=1, source_target_pairs={{0,4},{4,0},{1,5},{5,1},{2,6},{6,2},{3,7},{7,3},{8,12},{12,8},{9,1... | collective-permute-start | bytes 25165832 | tf_op jit(solution)/shard_map/ppermute | solution.py:60
  45.9 16.0 %collective-permute-start.4 = (bf16[256,1024]{1,0:T(8,128)(2,1)}, bf16[256,1024]{1,0:T(8,128)(2,1)}, u32[]{:S(2)}, u32[]{:S(2)}) collective-permute-start(bf16[256,1024]{1,0:T(8,128)(2,1)} %param.7), channel_id=1, source_target_pairs={{0,1},{1,2},{2,3},{3,0},{4,5},{5,6},{6,7},{7,4},{8,9},{9,10},{10,1... | collective-permute-start | bytes 1572872 | tf_op jit(solution)/shard_map/ppermute | solution.py:22
  47.9 24.8 %collective-permute-start.5 = (bf16[256,1024]{1,0:T(8,128)(2,1)}, bf16[256,1024]{1,0:T(8,128)(2,1)}, u32[]{:S(2)}, u32[]{:S(2)}) collective-permute-start(bf16[256,1024]{1,0:T(8,128)(2,1)} %param.7), channel_id=1, source_target_pairs={{0,2},{1,3},{2,0},{3,1},{4,6},{5,7},{6,4},{7,5},{8,10},{9,11},{10,... | collective-permute-start | bytes 1572872 | tf_op jit(solution)/shard_map/ppermute | solution.py:22
  48.3 26.3 %collective-permute-start.6 = (bf16[256,1024]{1,0:T(8,128)(2,1)}, bf16[256,1024]{1,0:T(8,128)(2,1)}, u32[]{:S(2)}, u32[]{:S(2)}) collective-permute-start(bf16[256,1024]{1,0:T(8,128)(2,1)} %param.7), channel_id=1, source_target_pairs={{0,3},{1,0},{2,1},{3,2},{4,7},{5,4},{6,5},{7,6},{8,11},{9,8},{10,9... | collective-permute-start | bytes 1572872 | tf_op jit(solution)/shard_map/ppermute | solution.py:22
  95.3 76.9 %copy-start = (bf16[128,4096]{1,0:T(8,128)(2,1)S(1)}, bf16[128,4096]{1,0:T(8,128)(2,1)}, u32[]{:S(2)}) copy-start(bf16[128,4096]{1,0:T(8,128)(2,1)} %param.9) | copy-start | bytes 3145732
  100.1 28.3 %collective-permute-start.7 = (bf16[128,4096]{1,0:T(8,128)(2,1)}, bf16[128,4096]{1,0:T(8,128)(2,1)}, u32[]{:S(2)}, u32[]{:S(2)}) collective-permute-start(bf16[128,4096]{1,0:T(8,128)(2,1)} %get-tuple-element.30), channel_id=1, source_target_pairs={{0,8},{8,16},{16,24},{24,0},{1,9},{9,17},{17,25},{25,1},{2,10},{10... | collective-permute-start | bytes 3145736 | tf_op jit(solution)/shard_map/ppermute | solution.py:69
  100.1 72.2 %collective-permute-start.9 = (bf16[128,4096]{1,0:T(8,128)(2,1)}, bf16[128,4096]{1,0:T(8,128)(2,1)}, u32[]{:S(2)}, u32[]{:S(2)}) collective-permute-start(bf16[128,4096]{1,0:T(8,128)(2,1)} %get-tuple-element.31), channel_id=1, source_target_pairs={{0,16},{8,24},{16,0},{24,8},{1,17},{9,25},{17,1},{25,9},{2,18},{10... | collective-permute-start | bytes 3145736 | tf_op jit(solution)/shard_map/ppermute | solution.py:69
  101.2 71.0 %collective-permute-start.8 = (bf16[128,4096]{1,0:T(8,128)(2,1)}, bf16[128,4096]{1,0:T(8,128)(2,1)}, u32[]{:S(2)}, u32[]{:S(2)}) collective-permute-start(bf16[128,4096]{1,0:T(8,128)(2,1)} %get-tuple-element.32), channel_id=1, source_target_pairs={{0,24},{8,0},{16,8},{24,16},{1,25},{9,1},{17,9},{25,17},{2,26},{10... | collective-permute-start | bytes 3145736 | tf_op jit(solution)/shard_map/ppermute | solution.py:69
  178.1 184.7 %all-gather.8.cloned.1.call-start = ((), (), s32[]{:S(2)}) async-start(), calls=%async_computation.2 | async-start | bytes 9437184 | tf_op jit(solution)/shard_map/all_gather | solution.py:80
  280.6 17.6 %copy-start.3 = (bf16[1024,4096]{1,0:T(8,128)(2,1)S(1)}, bf16[1024,4096]{1,0:T(8,128)(2,1)}, u32[]{:S(2)}) copy-start(bf16[1024,4096]{1,0:T(8,128)(2,1)} %all-gather.6.cloned.1.call-done) | copy-start | bytes 25165828
  293.7 27.0 %collective-permute-start.10 = (f32[256,1024]{1,0:T(8,128)S(1)}, f32[256,1024]{1,0:T(8,128)S(1)}, u32[]{:S(2)}, u32[]{:S(2)}) collective-permute-start(f32[256,1024]{1,0:T(8,128)S(1)} %get-tuple-element.36), channel_id=1, source_target_pairs={{0,1},{1,2},{2,3},{3,0},{4,5},{5,6},{6,7},{7,4},{8,9},{9,10},{10,1... | collective-permute-start | bytes 3145736 | tf_op jit(solution)/shard_map/ppermute | solution.py:34
  295.3 47.3 %collective-permute-start.12 = (f32[256,1024]{1,0:T(8,128)S(1)}, f32[256,1024]{1,0:T(8,128)S(1)}, u32[]{:S(2)}, u32[]{:S(2)}) collective-permute-start(f32[256,1024]{1,0:T(8,128)S(1)} %get-tuple-element.37), channel_id=1, source_target_pairs={{0,3},{1,0},{2,1},{3,2},{4,7},{5,4},{6,5},{7,6},{8,11},{9,8},{10,9... | collective-permute-start | bytes 3145736 | tf_op jit(solution)/shard_map/ppermute | solution.py:34
  296.7 45.9 %collective-permute-start.11 = (f32[256,1024]{1,0:T(8,128)S(1)}, f32[256,1024]{1,0:T(8,128)S(1)}, u32[]{:S(2)}, u32[]{:S(2)}) collective-permute-start(f32[256,1024]{1,0:T(8,128)S(1)} %get-tuple-element.38), channel_id=1, source_target_pairs={{0,2},{1,3},{2,0},{3,1},{4,6},{5,7},{6,4},{7,5},{8,10},{9,11},{10,... | collective-permute-start | bytes 3145736 | tf_op jit(solution)/shard_map/ppermute | solution.py:34
  375.5 20.3 %slice-start = ((s8[16777216]{0:T(1024)(128)(4,1)}), s8[4194304]{0:T(1024)(128)(4,1)S(1)}, s32[]{:S(2)}) async-start(s8[16777216]{0:T(1024)(128)(4,1)} %bitcast.61), calls=%async_computation.3 | async-start | bytes 8388608
  375.8 24.1 %collective-permute-start.13 = (bf16[256,1024]{1,0:T(8,128)(2,1)S(1)}, bf16[256,1024]{1,0:T(8,128)(2,1)S(1)}, u32[]{:S(2)}, u32[]{:S(2)}) collective-permute-start(bf16[256,1024]{1,0:T(8,128)(2,1)S(1)} %get-tuple-element.33), channel_id=1, source_target_pairs={{0,1},{1,2},{2,3},{3,0},{4,5},{5,6},{6,7},{7,4},{8,9},{9,10},{10,1... | collective-permute-start | bytes 1572872 | tf_op jit(solution)/shard_map/ppermute | solution.py:34
  377.3 24.8 %collective-permute-start.15 = (bf16[256,1024]{1,0:T(8,128)(2,1)S(1)}, bf16[256,1024]{1,0:T(8,128)(2,1)S(1)}, u32[]{:S(2)}, u32[]{:S(2)}) collective-permute-start(bf16[256,1024]{1,0:T(8,128)(2,1)S(1)} %get-tuple-element.34), channel_id=1, source_target_pairs={{0,3},{1,0},{2,1},{3,2},{4,7},{5,4},{6,5},{7,6},{8,11},{9,8},{10,9... | collective-permute-start | bytes 1572872 | tf_op jit(solution)/shard_map/ppermute | solution.py:34
  378.7 17.1 %slice-start.1 = ((s8[16777216]{0:T(1024)(128)(4,1)}), s8[4194304]{0:T(1024)(128)(4,1)S(1)}, s32[]{:S(2)}) async-start(s8[16777216]{0:T(1024)(128)(4,1)} %bitcast.61), calls=%async_computation.4 | async-start | bytes 8388608
  378.7 17.1 %slice-start.2 = ((s8[16777216]{0:T(1024)(128)(4,1)}), s8[4194304]{0:T(1024)(128)(4,1)S(1)}, s32[]{:S(2)}) async-start(s8[16777216]{0:T(1024)(128)(4,1)} %bitcast.61), calls=%async_computation.5 | async-start | bytes 8388608
  378.7 17.1 %slice-start.3 = ((s8[16777216]{0:T(1024)(128)(4,1)}), s8[4194304]{0:T(1024)(128)(4,1)S(1)}, s32[]{:S(2)}) async-start(s8[16777216]{0:T(1024)(128)(4,1)} %bitcast.61), calls=%async_computation.6 | async-start | bytes 8388608
  378.7 23.4 %collective-permute-start.14 = (bf16[256,1024]{1,0:T(8,128)(2,1)S(1)}, bf16[256,1024]{1,0:T(8,128)(2,1)S(1)}, u32[]{:S(2)}, u32[]{:S(2)}) collective-permute-start(bf16[256,1024]{1,0:T(8,128)(2,1)S(1)} %get-tuple-element.35), channel_id=1, source_target_pairs={{0,2},{1,3},{2,0},{3,1},{4,6},{5,7},{6,4},{7,5},{8,10},{9,11},{10,... | collective-permute-start | bytes 1572872 | tf_op jit(solution)/shard_map/ppermute | solution.py:34
Sparse Core Ops, SparseCore 0:
  10.6 84.7 all-gather.3
  178.2 102.3 all-gather.5
  282.2 80.5 all-gather.7
where the time goes:
time: 410 us
  waiting for transfers between devices  250 us (61%)
  matrix products  87.6 us (21%)
  starting transfers between devices  23.8 us (6%)
  other arithmetic  17.8 us (4%)
  local copies, waits for them, and re-layouts  17.1 us (4%)
  between operations  14 us (3%)
    all_gather x1, waiting for transfers between devices, body(): gate_delta = lax.all_gather(gate_local, ROW, axis=0, tiled=True)  84.4 us
    ppermute x3, waiting for transfers between devices, body(): piece = lax.ppermute(piece.astype(jnp.bfloat16), 'z', shift_perm(chips, s))  68.3 us
    ppermute x6, waiting for transfers between devices, gather_col(): part = lax.ppermute(block, 'col', shift_perm(n, s))  36.6 us
    ppermute x6, waiting for transfers between devices, reduce_scatter_col(): piece = lax.ppermute(piece.astype(send_dtype), 'col', shift_perm(n, s))  32.9 us
    all_gather x1, waiting for transfers between devices, body(): up_delta = lax.all_gather(up_local, ROW, axis=0, tiled=True)  19.9 us
    dot_general x1, matrix products, body(): lax.dot_general(act_full, up_delta, CONTRACT_FIRST, preferred_element_typ...  15.6 us
    dot_general x1, matrix products, body(): lax.dot_general(hidden_act, grad_full, CONTRACT_FIRST, preferred_element_...  14.6 us
    dot_general x1, matrix products, body(): lax.dot_general(act_full, gate_delta, CONTRACT_FIRST, preferred_element_t...  13.7 us
  transfers between devices with their start and end apart: 19, of which 12 were waited for; matrix products, arithmetic and copies ran while one was open for 23% of the time, Pallas kernels for 0%

commit v1 on v0

--- a/solution.py
+++ b/solution.py
@@ -76,8 +76,11 @@
     acc_down = lax.dot_general(
         hidden_act, grad_full, CONTRACT_FIRST, preferred_element_type=jnp.float32
     )
-    gate_delta = lax.all_gather(gate_local, ROW, axis=0, tiled=True)
-    up_delta = lax.all_gather(up_local, ROW, axis=0, tiled=True)
+    gate_delta, up_delta = jnp.split(
+        lax.all_gather(jnp.concatenate([gate_local, up_local], axis=1), ROW, axis=0, tiled=True),
+        [gate_local.shape[1]],
+        axis=1,
+    )
     acc_gate = lax.dot_general(
         act_full, gate_delta, CONTRACT_FIRST, preferred_element_type=jnp.float32
     )

time: 410 us -> 464 us (1.13)
  waiting for transfers between devices: 250 us -> 296 us
  local copies, waits for them, and re-layouts: 17.1 us -> 27.2 us
    all_gather x2 -> x1, waiting for transfers between devices: 104 us -> 157 us  [body(): lax.all_gather(jnp.concatenate([gate_local, up_local], axis=1), ROW, axis...]
    split x0 -> x1, local copies, waits for them, and re-layouts: none -> 7.89 us  [body(): jnp.split(lax.all_gather(jnp.concatenate([gate_local, up_local], axis=1),...]
    ppermute x6, waiting for transfers between devices: 32.9 us -> 27.1 us  [reduce_scatter_col(): piece = lax.ppermute(piece.astype(send_dtype), 'col', shift_perm(n, s))]
  transfers between devices with their start and end apart: 19 -> 18, of which waited for: 12 -> 11; matrix products, arithmetic and copies ran while one was open for 23% -> 18% of each run, Pallas kernels for 0% -> 0%
where the time goes in v1:
time: 464 us; the launch traced here: 463 us
  waiting for transfers between devices  296 us (64%)
  matrix products  85.5 us (18%)
  local copies, waits for them, and re-layouts  27.2 us (6%)
  starting transfers between devices  23.4 us (5%)
  other arithmetic  16.5 us (4%)
  between operations  14.2 us (3%)
    all_gather x1, waiting for transfers between devices, body(): lax.all_gather(jnp.concatenate([gate_local, up_local], axis=1), ROW, axis...  157 us
    ppermute x3, waiting for transfers between devices, body(): piece = lax.ppermute(piece.astype(jnp.bfloat16), 'z', shift_perm(chips, s))  68.3 us
    ppermute x6, waiting for transfers between devices, gather_col(): part = lax.ppermute(block, 'col', shift_perm(n, s))  36.4 us
    ppermute x6, waiting for transfers between devices, reduce_scatter_col(): piece = lax.ppermute(piece.astype(send_dtype), 'col', shift_perm(n, s))  27.1 us
    dot_general x1, matrix products, body(): lax.dot_general(act_full, up_delta, CONTRACT_FIRST, preferred_element_typ...  14.9 us
    dot_general x1, matrix products, body(): lax.dot_general(hidden_act, grad_full, CONTRACT_FIRST, preferred_element_...  14.6 us
    dot_general x1, matrix products, body(): lax.dot_general(gate_delta, gate_weight, CONTRACT_LAST, preferred_element...  12.7 us
    dot_general x1, matrix products, body(): lax.dot_general(up_delta, up_weight, CONTRACT_LAST, preferred_element_typ...  12.6 us
  transfers between devices with their start and end apart: 18, of which 11 were waited for; matrix products, arithmetic and copies ran while one was open for 18% of the time, Pallas kernels for 0%

profile of v1, /device:TPU:0, one launch (start us, length us, event | category | flops | bytes accessed | tf_op | source)
XLA Modules:
  0.0 463.1 jit_solution(10371404103566476740)
XLA Ops:
  7.2 3.2 fusion.4
  10.5 3.0 collective-permute-start
  16.8 10.6 %collective-permute-done = bf16[256,1024]{1,0:T(8,128)(2,1)} collective-permute-done((bf16[256,1024]{1,0:T(8,128)(2,1)S(1)}, bf16[256,1024]{1,0:T(8,128)(2,1)}, u32[]{:S(2)}, u32[]{:S(2)}) %collective-permute-start) | collective-permute-done | bytes 524320 | tf_op jit(solution)/shard_map/ppermute | solution.py:22
  28.4 9.3 %collective-permute-done.1 = bf16[256,1024]{1,0:T(8,128)(2,1)} collective-permute-done((bf16[256,1024]{1,0:T(8,128)(2,1)S(1)}, bf16[256,1024]{1,0:T(8,128)(2,1)}, u32[]{:S(2)}, u32[]{:S(2)}) %collective-permute-start.1) | collective-permute-done | bytes 524320 | tf_op jit(solution)/shard_map/ppermute | solution.py:22
  39.1 6.8 %fusion.27 = f32[512,4096]{1,0:T(8,128)} fusion(bf16[512,1024]{1,0:T(8,128)(2,1)S(1)} %bitcast.67, bf16[4096,1024]{1,0:T(8,128)(2,1)S(1)} %copy-done.3), kind=kOutput, calls=%fused_computation.59 | convolution fusion | flops 4294967296 | bytes 17825792 | tf_op jit(solution)/shard_map/dot_general | solution.py:57
  45.9 2.0 collective-permute-start.4
  48.3 2.3 collective-permute-start.6
  52.2 2.0 constant_dynamic-update-slice_fusion.3
  54.2 7.7 %collective-permute-done.4 = bf16[256,1024]{1,0:T(8,128)(2,1)} collective-permute-done((bf16[256,1024]{1,0:T(8,128)(2,1)}, bf16[256,1024]{1,0:T(8,128)(2,1)}, u32[]{:S(2)}, u32[]{:S(2)}) %collective-permute-start.4) | collective-permute-done | bytes 524320 | tf_op jit(solution)/shard_map/ppermute | solution.py:22
  61.9 1.9 constant_dynamic-update-slice_fusion.2
  63.8 8.9 %collective-permute-done.5 = bf16[256,1024]{1,0:T(8,128)(2,1)} collective-permute-done((bf16[256,1024]{1,0:T(8,128)(2,1)}, bf16[256,1024]{1,0:T(8,128)(2,1)}, u32[]{:S(2)}, u32[]{:S(2)}) %collective-permute-start.5) | collective-permute-done | bytes 524320 | tf_op jit(solution)/shard_map/ppermute | solution.py:22
  72.7 1.9 constant_dynamic-update-slice_fusion.1
  76.4 11.5 %convolution_add_fusion = f32[512,4096]{1,0:T(8,128)} fusion(f32[512,4096]{1,0:T(8,128)} %collective-permute-done.3, bf16[512,1024]{1,0:T(8,128)(2,1)S(1)} %bitcast.66, bf16[4096,1024]{1,0:T(8,128)(2,1)} %param.13), kind=kOutput, calls=%fused_computation.7 | convolution fusion | flops 4297064448 | bytes 26214400 | tf_op jit(solution)/shard_map/dot_general | solution.py:61
  88.0 7.4 %all-gather.3.cloned.1.call-done = bf16[1024,4096]{1,0:T(8,128)(2,1)} async-done(((bf16[128,4096]{1,0:T(8,128)(2,1)}), bf16[1024,4096]{1,0:T(8,128)(2,1)}) %all-gather.3.cloned.1.call-update) | async-done | bytes 8388624 | tf_op jit(solution)/shard_map/all_gather | solution.py:45
  95.3 4.7 %fusion.14 = (bf16[128,4096]{1,0:T(8,128)(2,1)}, bf16[128,4096]{1,0:T(8,128)(2,1)}, bf16[128,4096]{1,0:T(8,128)(2,1)}) fusion(f32[4,128,4096]{2,1,0:T(8,128)} %bitcast.62, s32[]{:T(128)S(6)} %select_n.115, s32[]{:T(128)S(6)} %select_n.119, s32[]{:T(128)S(6)} %select_n.117), kind=kLoop, calls=%fused_computation.29 | loop fusion | bytes 6291468 | tf_op jit(solution)/shard_map/convert_element_type | solution.py:69
  101.3 2.7 collective-permute-start.8
  104.0 24.4 %collective-permute-done.7 = bf16[128,4096]{1,0:T(8,128)(2,1)} collective-permute-done((bf16[128,4096]{1,0:T(8,128)(2,1)}, bf16[128,4096]{1,0:T(8,128)(2,1)}, u32[]{:S(2)}, u32[]{:S(2)}) %collective-permute-start.7) | collective-permute-done | bytes 1048608 | tf_op jit(solution)/shard_map/ppermute | solution.py:69
  128.4 43.9 %collective-permute-done.9 = bf16[128,4096]{1,0:T(8,128)(2,1)} collective-permute-done((bf16[128,4096]{1,0:T(8,128)(2,1)}, bf16[128,4096]{1,0:T(8,128)(2,1)}, u32[]{:S(2)}, u32[]{:S(2)}) %collective-permute-start.9) | collective-permute-done | bytes 1048608 | tf_op jit(solution)/shard_map/ppermute | solution.py:69
  172.3 4.2 fusion.7
  178.6 14.6 %multiply_convert_fusion = bf16[4096,1024]{1,0:T(8,128)(2,1)} fusion(bf16[1024,4096]{1,0:T(8,128)(2,1)} %all-gather.3.cloned.1.call-done, bf16[1024,1024]{1,0:T(8,128)(2,1)S(1)} %constant_dynamic-update-slice_fusion.4), kind=kOutput, calls=%fused_computation | convolution fusion | flops 8598323200 | bytes 18874368 | tf_op jit(solution)/shard_map/dot_general | solution.py:76
  193.2 156.9 %all-gather.5.cloned.1.call-done = bf16[1024,8192]{1,0:T(8,128)(2,1)} async-done(((bf16[128,8192]{1,0:T(8,128)(2,1)}), bf16[1024,8192]{1,0:T(8,128)(2,1)}) %all-gather.5.cloned.1.call-update) | async-done | bytes 16777232 | tf_op jit(solution)/shard_map/all_gather | solution.py:80
  350.1 12.7 %fusion = f32[1024,1024]{1,0:T(8,128)S(1)} fusion(bf16[1024,4096]{1,0:T(8,128)(2,1)} %param.11, bf16[1024,8192]{1,0:T(8,128)(2,1)} %all-gather.5.cloned.1.call-done), kind=kOutput, calls=%fused_computation.3 | convolution fusion | flops 8589934592 | bytes 20971520 | tf_op jit(solution)/shard_map/dot_general | solution.py:88
  369.5 7.9 %split.9 = bf16[1024,4096]{1,0:T(8,128)(2,1)} slice(bf16[1024,8192]{1,0:T(8,128)(2,1)} %all-gather.5.cloned.1.call-done), slice={[0:1024], [4096:8192]} | slice | bytes 16777216 | tf_op jit(solution)/shard_map/split | solution.py:79
  377.4 12.4 %fusion.2 = f32[1024,4096]{1,0:T(8,128)S(1)} fusion(bf16[1024,1024]{1,0:T(8,128)(2,1)} %constant_dynamic-update-slice_fusion, bf16[1024,8192]{1,0:T(8,128)(2,1)} %all-gather.5.cloned.1.call-done), kind=kOutput, calls=%fused_computation.5 | convolution fusion | flops 8589934592 | bytes 27262976 | tf_op jit(solution)/shard_map/dot_general | solution.py:84
  389.8 2.5 collective-permute-done.10
  392.3 21.8 %collective-permute-done.12 = f32[256,1024]{1,0:T(8,128)S(1)} collective-permute-done((f32[256,1024]{1,0:T(8,128)S(1)}, f32[256,1024]{1,0:T(8,128)S(1)}, u32[]{:S(2)}, u32[]{:S(2)}) %collective-permute-start.12) | collective-permute-done | bytes 1048608 | tf_op jit(solution)/shard_map/ppermute | solution.py:34
  414.1 1.9 fusion.22
  416.1 12.6 %fusion.28 = f32[1024,1024]{1,0:T(8,128)S(1)} fusion(bf16[1024,4096]{1,0:T(8,128)(2,1)} %split.9, bf16[1024,4096]{1,0:T(8,128)(2,1)} %param.12), kind=kOutput, calls=%fused_computation.60 | convolution fusion | flops 8589934592 | bytes 20971520 | tf_op jit(solution)/shard_map/dot_general | solution.py:91
  429.0 1.9 collective-permute-start.13
  433.4 14.9 %multiply_convert_fusion.1 = bf16[1024,4096]{1,0:T(8,128)(2,1)} fusion(bf16[1024,1024]{1,0:T(8,128)(2,1)} %constant_dynamic-update-slice_fusion, bf16[1024,4096]{1,0:T(8,128)(2,1)} %split.9), kind=kOutput, calls=%fused_computation.1 | convolution fusion | flops 8598323200 | bytes 18874368 | tf_op jit(solution)/shard_map/dot_general | solution.py:96
  448.4 4.0 multiply_convert_fusion.2
  452.3 2.8 collective-permute-done.15
  (43 shorter events, 23.7 us)
Async XLA Ops:
  7.2 3.3 copy-start.2
  7.2 88.2 %all-gather.3.cloned.1.call-start = ((), (), s32[]{:S(2)}) async-start(), calls=%async_computation | async-start | bytes 9437184 | tf_op jit(solution)/shard_map/all_gather | solution.py:45
  10.4 339.7 %all-gather.5.cloned.1.call-start = ((), (), s32[]{:S(2)}) async-start(), calls=%async_computation.1 | async-start | bytes 18874368 | tf_op jit(solution)/shard_map/all_gather | solution.py:80
  10.5 16.8 %collective-permute-start = (bf16[256,1024]{1,0:T(8,128)(2,1)S(1)}, bf16[256,1024]{1,0:T(8,128)(2,1)}, u32[]{:S(2)}, u32[]{:S(2)}) collective-permute-start(bf16[256,1024]{1,0:T(8,128)(2,1)S(1)} %copy-done.2), channel_id=1, source_target_pairs={{0,1},{1,2},{2,3},{3,0},{4,5},{5,6},{6,7},{7,4},{8,9},{9,10},{10,1... | collective-permute-start | bytes 1572872 | tf_op jit(solution)/shard_map/ppermute | solution.py:22
  13.5 24.2 %collective-permute-start.1 = (bf16[256,1024]{1,0:T(8,128)(2,1)S(1)}, bf16[256,1024]{1,0:T(8,128)(2,1)}, u32[]{:S(2)}, u32[]{:S(2)}) collective-permute-start(bf16[256,1024]{1,0:T(8,128)(2,1)S(1)} %copy-done.2), channel_id=1, source_target_pairs={{0,2},{1,3},{2,0},{3,1},{4,6},{5,7},{6,4},{7,5},{8,10},{9,11},{10,... | collective-permute-start | bytes 1572872 | tf_op jit(solution)/shard_map/ppermute | solution.py:22
  15.0 23.8 %collective-permute-start.2 = (bf16[256,1024]{1,0:T(8,128)(2,1)S(1)}, bf16[256,1024]{1,0:T(8,128)(2,1)S(1)}, u32[]{:S(2)}, u32[]{:S(2)}) collective-permute-start(bf16[256,1024]{1,0:T(8,128)(2,1)S(1)} %copy-done.2), channel_id=1, source_target_pairs={{0,3},{1,0},{2,1},{3,2},{4,7},{5,4},{6,5},{7,6},{8,11},{9,8},{10,9... | collective-permute-start | bytes 1572872 | tf_op jit(solution)/shard_map/ppermute | solution.py:22
  16.7 22.4 %copy-start.3 = (bf16[4096,1024]{1,0:T(8,128)(2,1)S(1)}, bf16[4096,1024]{1,0:T(8,128)(2,1)}, u32[]{:S(2)}) copy-start(bf16[4096,1024]{1,0:T(8,128)(2,1)} %param.13) | copy-start | bytes 25165828
  45.9 30.5 %collective-permute-start.3 = (f32[512,4096]{1,0:T(8,128)}, f32[512,4096]{1,0:T(8,128)}, u32[]{:S(2)}, u32[]{:S(2)}) collective-permute-start(f32[512,4096]{1,0:T(8,128)} %fusion.27), channel_id=1, source_target_pairs={{0,4},{4,0},{1,5},{5,1},{2,6},{6,2},{3,7},{7,3},{8,12},{12,8},{9,1... | collective-permute-start | bytes 25165832 | tf_op jit(solution)/shard_map/ppermute | solution.py:60
  45.9 16.0 %collective-permute-start.4 = (bf16[256,1024]{1,0:T(8,128)(2,1)}, bf16[256,1024]{1,0:T(8,128)(2,1)}, u32[]{:S(2)}, u32[]{:S(2)}) collective-permute-start(bf16[256,1024]{1,0:T(8,128)(2,1)} %param.7), channel_id=1, source_target_pairs={{0,1},{1,2},{2,3},{3,0},{4,5},{5,6},{6,7},{7,4},{8,9},{9,10},{10,1... | collective-permute-start | bytes 1572872 | tf_op jit(solution)/shard_map/ppermute | solution.py:22
  47.9 24.8 %collective-permute-start.5 = (bf16[256,1024]{1,0:T(8,128)(2,1)}, bf16[256,1024]{1,0:T(8,128)(2,1)}, u32[]{:S(2)}, u32[]{:S(2)}) collective-permute-start(bf16[256,1024]{1,0:T(8,128)(2,1)} %param.7), channel_id=1, source_target_pairs={{0,2},{1,3},{2,0},{3,1},{4,6},{5,7},{6,4},{7,5},{8,10},{9,11},{10,... | collective-permute-start | bytes 1572872 | tf_op jit(solution)/shard_map/ppermute | solution.py:22
  48.3 26.3 %collective-permute-start.6 = (bf16[256,1024]{1,0:T(8,128)(2,1)}, bf16[256,1024]{1,0:T(8,128)(2,1)}, u32[]{:S(2)}, u32[]{:S(2)}) collective-permute-start(bf16[256,1024]{1,0:T(8,128)(2,1)} %param.7), channel_id=1, source_target_pairs={{0,3},{1,0},{2,1},{3,2},{4,7},{5,4},{6,5},{7,6},{8,11},{9,8},{10,9... | collective-permute-start | bytes 1572872 | tf_op jit(solution)/shard_map/ppermute | solution.py:22
  95.3 77.0 %copy-start = (bf16[128,4096]{1,0:T(8,128)(2,1)S(1)}, bf16[128,4096]{1,0:T(8,128)(2,1)}, u32[]{:S(2)}) copy-start(bf16[128,4096]{1,0:T(8,128)(2,1)} %param.9) | copy-start | bytes 3145732
  100.1 28.3 %collective-permute-start.7 = (bf16[128,4096]{1,0:T(8,128)(2,1)}, bf16[128,4096]{1,0:T(8,128)(2,1)}, u32[]{:S(2)}, u32[]{:S(2)}) collective-permute-start(bf16[128,4096]{1,0:T(8,128)(2,1)} %get-tuple-element.30), channel_id=1, source_target_pairs={{0,8},{8,16},{16,24},{24,0},{1,9},{9,17},{17,25},{25,1},{2,10},{10... | collective-permute-start | bytes 3145736 | tf_op jit(solution)/shard_map/ppermute | solution.py:69
  100.1 72.2 %collective-permute-start.9 = (bf16[128,4096]{1,0:T(8,128)(2,1)}, bf16[128,4096]{1,0:T(8,128)(2,1)}, u32[]{:S(2)}, u32[]{:S(2)}) collective-permute-start(bf16[128,4096]{1,0:T(8,128)(2,1)} %get-tuple-element.31), channel_id=1, source_target_pairs={{0,16},{8,24},{16,0},{24,8},{1,17},{9,25},{17,1},{25,9},{2,18},{10... | collective-permute-start | bytes 3145736 | tf_op jit(solution)/shard_map/ppermute | solution.py:69
  101.3 71.0 %collective-permute-start.8 = (bf16[128,4096]{1,0:T(8,128)(2,1)}, bf16[128,4096]{1,0:T(8,128)(2,1)}, u32[]{:S(2)}, u32[]{:S(2)}) collective-permute-start(bf16[128,4096]{1,0:T(8,128)(2,1)} %get-tuple-element.32), channel_id=1, source_target_pairs={{0,24},{8,0},{16,8},{24,16},{1,25},{9,1},{17,9},{25,17},{2,26},{10... | collective-permute-start | bytes 3145736 | tf_op jit(solution)/shard_map/ppermute | solution.py:69
  362.8 2.3 copy-start.1
  365.1 27.1 %collective-permute-start.10 = (f32[256,1024]{1,0:T(8,128)}, f32[256,1024]{1,0:T(8,128)S(1)}, u32[]{:S(2)}, u32[]{:S(2)}) collective-permute-start(f32[256,1024]{1,0:T(8,128)} %get-tuple-element.36), channel_id=1, source_target_pairs={{0,1},{1,2},{2,3},{3,0},{4,5},{5,6},{6,7},{7,4},{8,9},{9,10},{10,1... | collective-permute-start | bytes 3145736 | tf_op jit(solution)/shard_map/ppermute | solution.py:34
  366.6 47.5 %collective-permute-start.12 = (f32[256,1024]{1,0:T(8,128)S(1)}, f32[256,1024]{1,0:T(8,128)S(1)}, u32[]{:S(2)}, u32[]{:S(2)}) collective-permute-start(f32[256,1024]{1,0:T(8,128)S(1)} %get-tuple-element.37), channel_id=1, source_target_pairs={{0,3},{1,0},{2,1},{3,2},{4,7},{5,4},{6,5},{7,6},{8,11},{9,8},{10,9... | collective-permute-start | bytes 3145736 | tf_op jit(solution)/shard_map/ppermute | solution.py:34
  368.1 46.1 %collective-permute-start.11 = (f32[256,1024]{1,0:T(8,128)S(1)}, f32[256,1024]{1,0:T(8,128)}, u32[]{:S(2)}, u32[]{:S(2)}) collective-permute-start(f32[256,1024]{1,0:T(8,128)S(1)} %get-tuple-element.38), channel_id=1, source_target_pairs={{0,2},{1,3},{2,0},{3,1},{4,6},{5,7},{6,4},{7,5},{8,10},{9,11},{10,... | collective-permute-start | bytes 3145736 | tf_op jit(solution)/shard_map/ppermute | solution.py:34
  429.0 23.4 %collective-permute-start.13 = (bf16[256,1024]{1,0:T(8,128)(2,1)S(1)}, bf16[256,1024]{1,0:T(8,128)(2,1)S(1)}, u32[]{:S(2)}, u32[]{:S(2)}) collective-permute-start(bf16[256,1024]{1,0:T(8,128)(2,1)S(1)} %get-tuple-element.33), channel_id=1, source_target_pairs={{0,1},{1,2},{2,3},{3,0},{4,5},{5,6},{6,7},{7,4},{8,9},{9,10},{10,1... | collective-permute-start | bytes 1572872 | tf_op jit(solution)/shard_map/ppermute | solution.py:34
  430.9 24.2 %collective-permute-start.15 = (bf16[256,1024]{1,0:T(8,128)(2,1)S(1)}, bf16[256,1024]{1,0:T(8,128)(2,1)S(1)}, u32[]{:S(2)}, u32[]{:S(2)}) collective-permute-start(bf16[256,1024]{1,0:T(8,128)(2,1)S(1)} %get-tuple-element.34), channel_id=1, source_target_pairs={{0,3},{1,0},{2,1},{3,2},{4,7},{5,4},{6,5},{7,6},{8,11},{9,8},{10,9... | collective-permute-start | bytes 1572872 | tf_op jit(solution)/shard_map/ppermute | solution.py:34
  432.1 23.0 %collective-permute-start.14 = (bf16[256,1024]{1,0:T(8,128)(2,1)S(1)}, bf16[256,1024]{1,0:T(8,128)(2,1)S(1)}, u32[]{:S(2)}, u32[]{:S(2)}) collective-permute-start(bf16[256,1024]{1,0:T(8,128)(2,1)S(1)} %get-tuple-element.35), channel_id=1, source_target_pairs={{0,2},{1,3},{2,0},{3,1},{4,6},{5,7},{6,4},{7,5},{8,10},{9,11},{10,... | collective-permute-start | bytes 1572872 | tf_op jit(solution)/shard_map/ppermute | solution.py:34
Sparse Core Ops, SparseCore 0:
  10.6 84.7 all-gather.2
  178.7 171.3 all-gather.4
